TPU v7x, 256 devices: a whole 4x4x8 slice. The times are simulated.
256 devices in a mesh: aa: 32 (over z, x), ba: 8 (over y, core).
Axes of the slice: x: 4, y: 4, z: 8, core: 2. Of those that a mesh axis runs over, the one named last changes fastest.
Arguments:
- snapshots: float32 [8192, 65536], P(('aa', 'ba')), may hold values from -125 to 125
Outputs:
- factors: float32 [8, 64, 64], replicated
- pod_modes: float32 [8, 64, 65536], P(None, None, ('aa', 'ba'))
All inputs are finite; a program needn't handle non-finite values.
Results may differ from a plain program's by a relative error of at most 0.000098.
Values sent between devices are 32-bit elements; how exact they have to be, the bound alone decides.
No kernel may reach another device: no remote copies, remote signals or barrier semaphores. Data moves between devices by JAX's collectives and lax.ppermute only.
A program may use at most 128 MiB of HBM per device.

v0:
```python
import math
import jax
import jax.numpy as jnp
from jax import lax
from jax.sharding import PartitionSpec as P

FREQS = 8


def spectral_rows(block_len, points, first, count):
    sample = first + jnp.arange(count, dtype=jnp.int32)
    harmonic = jnp.arange(1, FREQS + 1, dtype=jnp.int32)
    phase_turns = (sample[:, None] * harmonic[None, :] % block_len).astype(jnp.float32) * (
        2.0 * math.pi / block_len
    )
    full = jnp.arange(block_len, dtype=jnp.int32).astype(jnp.float32) * (2.0 * math.pi / block_len)
    full_window = 0.5 - 0.5 * jnp.cos(full)
    norm_scale = 1.0 / jnp.sqrt(points * jnp.sum(full_window * full_window))
    sample_angle = sample.astype(jnp.float32) * (2.0 * math.pi / block_len)
    window = 0.5 - 0.5 * jnp.cos(sample_angle)
    cosine = window[:, None] * jnp.cos(phase_turns) * norm_scale
    sine = -window[:, None] * jnp.sin(phase_turns) * norm_scale
    return jnp.stack([cosine, sine], axis=1)


def local(snapshots):
    time_dev, points = snapshots.shape
    n_aa = lax.axis_size("aa")
    n_ba = lax.axis_size("ba")
    pts_dev = points // (n_aa * n_ba)
    block_len = time_dev * n_ba
    u = lax.axis_index("ba")
    table = spectral_rows(block_len, points, u * time_dev, time_dev)
    arranged = snapshots.reshape(time_dev, n_aa, n_ba, pts_dev)
    partial = jnp.einsum("savq,sgf->vgfaq", arranged, table, precision=lax.Precision.HIGHEST)
    block_spec = lax.psum_scatter(partial, "ba", scatter_dimension=0, tiled=True)
    spectra = lax.all_to_all(block_spec, "aa", split_axis=3, concat_axis=0, tiled=True)
    blocks = spectra.shape[0]
    columns = 2 * blocks
    cols = jnp.transpose(spectra.reshape(blocks, 2, FREQS, pts_dev), (2, 0, 1, 3)).reshape(
        FREQS, columns, pts_dev
    )
    product = jnp.einsum("fip,fjp->fij", cols, cols, precision=lax.Precision.HIGHEST)
    gram_sum = lax.psum(product, ("aa", "ba"))
    lower_factor = jnp.linalg.cholesky(gram_sum)
    identity = jnp.broadcast_to(jnp.eye(columns, dtype=gram_sum.dtype), lower_factor.shape)
    inverse = lax.linalg.triangular_solve(lower_factor, identity, left_side=True, lower=True)
    pod_modes = math.sqrt(points) * jnp.einsum(
        "fij,fjp->fip", inverse, cols, precision=lax.Precision.HIGHEST
    )
    return (jnp.swapaxes(lower_factor, 1, 2), pod_modes)


def solution(mesh):
    placed = (P(("aa", "ba"), None),)
    return jax.shard_map(
        local,
        mesh=mesh,
        in_specs=placed,
        out_specs=(P(), P(None, None, ("aa", "ba"))),
        check_vma=False,
    )
```

profile of v0, /device:TPU:2, one launch (start us, length us, event | category | flops | bytes accessed | tf_op | source)
XLA Modules:
  0.0 479.1 jit_solution(12910174082356562652)
XLA Ops:
  7.2 0.0 all-reduce.6.cloned.1.call-start
  7.3 0.6 multiply_reduce_fusion
  8.6 5.9 %copy.38 = f32[4,8,256,256]{3,2,1,0:T(8,128)S(1)} copy(f32[4,8,256,256]{3,1,2,0:T(8,128)} %bitcast.42) | data formatting | bytes 16777216
  14.6 0.1 multiply_multiply_fusion.1
  14.7 9.2 %fusion.3 = f32[8,2,8,32,256]{4,2,0,3,1:T(8,128)} fusion(f32[32,32,8,256]{3,2,1,0:T(8,128)S(1)} %bitcast.41, f32[32,1,8]{0,2,1:T(8,128)S(1)} %get-tuple-element.13, f32[32,1,8]{0,2,1:T(8,128)S(1)} %get-tuple-element.12), kind=kOutput, calls=%fused_computation.3 | convolution fusion | flops 402653696 | bytes 12584960 | tf_op jit(solution)/shard_map/savq,sgf->vgfaq/dot_general | solution.py:35
  23.9 0.0 all-reduce.6.cloned.1.call-update
  23.9 0.6 dynamic-slice
  24.5 80.1 %all-reduce.6.cloned.1.call-done = f32[8,2,8,32,256]{4,2,0,3,1:T(8,128)} async-done(((f32[8,2,8,32,256]{4,2,0,3,1:T(8,128)}), f32[8,2,8,32,256]{4,2,0,3,1:T(8,128)}) %all-reduce.6.cloned.1.call-update) | async-done | bytes 4194320
  104.6 1.7 constant_dynamic-slice_fusion
  106.3 0.9 copy.25
  107.2 10.1 %all-to-all-start = ((f32[1,2,8,32,256]{4,2,0,1,3:T(8,128)}), f32[1,2,8,32,256]{4,2,0,1,3:T(8,128)S(1)}, u32[]{:S(2)}, u32[]{:S(2)}) async-start(f32[1,2,8,32,256]{4,2,0,1,3:T(8,128)} %copy.25), calls=%async_computation | async-start | bytes 1048576 | tf_op jit(solution)/shard_map/all_to_all | solution.py:37
  117.3 0.2 all-reduce.4.cloned.1.call-start
  117.6 14.8 %all-to-all-done = f32[1,2,8,32,256]{4,2,0,1,3:T(8,128)S(1)} async-done(((f32[1,2,8,32,256]{4,2,0,1,3:T(8,128)}), f32[1,2,8,32,256]{4,2,0,1,3:T(8,128)S(1)}, u32[]{:S(2)}, u32[]{:S(2)}) %all-to-all-start) | async-done | bytes 524320 | tf_op jit(solution)/shard_map/all_to_all | solution.py:37
  132.4 1.6 fusion.7
  134.0 246.7 %all-reduce.4.cloned.1.call-done = f32[8,64,64]{1,2,0:T(8,128)} async-done(((f32[8,64,64]{1,2,0:T(8,128)}), f32[8,64,64]{1,2,0:T(8,128)}) %all-reduce.4.cloned.1.call-update) | async-done | bytes 131088 | tf_op jit(solution)/shard_map/psum | solution.py:44
  380.7 1.1 copy.29
  381.8 1.0 fusion.11
  382.8 46.9 %custom-call.7 = f32[8,64,64]{2,1,0:T(8,128)S(1)} custom-call(f32[8,64,64]{2,1,0:T(8,128)S(1)} %fusion.11), custom_call_target="Cholesky" | custom-call | tf_op jit(solution)/shard_map/jit(cholesky)/cholesky | solution.py:45
  429.8 0.1 compare_reduce_fusion
  429.9 0.1 select_bitcast_fusion
  430.0 39.3 %custom-call.8 = f32[8,1,64,64]{2,3,1,0:T(8,128)S(1)} custom-call(f32[8,1,64,64]{3,2,1,0:T(8,128)S(1)} %get-tuple-element.10), custom_call_target="InvertDiagBlocksLowerTriangular" | custom-call | tf_op jit(solution)/shard_map/triangular_solve | solution.py:47
  469.3 0.6 fusion.9
  469.9 1.5 convolution_multiply_fusion
  471.5 0.8 copy.32
  (10 shorter events, 0.1 us)
Async XLA Ops:
  7.2 97.5 %all-reduce.6.cloned.1.call-start = ((), (), s32[]{:S(2)}) async-start(), calls=%async_computation.2 | async-start | bytes 8388608
  14.7 9.2 %copy-start = (u32[256]{0:T(256)S(1)}, u32[256]{0:T(256)}, u32[]{:S(2)}) copy-start(u32[256]{0:T(256)} %constant.81) | copy-start | bytes 3076
  107.2 25.2 %all-to-all-start = ((f32[1,2,8,32,256]{4,2,0,1,3:T(8,128)}), f32[1,2,8,32,256]{4,2,0,1,3:T(8,128)S(1)}, u32[]{:S(2)}, u32[]{:S(2)}) async-start(f32[1,2,8,32,256]{4,2,0,1,3:T(8,128)} %copy.25), calls=%async_computation | async-start | bytes 1048576 | tf_op jit(solution)/shard_map/all_to_all | solution.py:37
  117.3 263.4 %all-reduce.4.cloned.1.call-start = ((), (), s32[]{:S(2)}) async-start(), calls=%async_computation.1 | async-start | bytes 524288 | tf_op jit(solution)/shard_map/psum | solution.py:44
Sparse Core Ops, SparseCore 0:
  24.0 80.5 all-reduce.5
  134.1 246.5 all-reduce.3
where the time goes:
time: 479 us
  waiting for transfers between devices  342 us (71%)
  other arithmetic  88.3 us (18%)
  between operations  14.8 us (3%)
  matrix products  12.9 us (3%)
  local copies, waits for them, and re-layouts  11 us (2%)
  starting transfers between devices  10.4 us (2%)
    psum x1, waiting for transfers between devices, local(): gram_sum = lax.psum(product, ('aa', 'ba'))  247 us
    unnamed x3, waiting for transfers between devices  80.2 us
    another operation x4, other arithmetic, local(): lower_factor = jnp.linalg.cholesky(gram_sum)  47.1 us
    another operation x2, other arithmetic, local(): lax.linalg.triangular_solve(lower_factor, identity, left_side=True, lower...  39.4 us
    all_to_all x1, waiting for transfers between devices, local(): lax.all_to_all(block_spec, 'aa', split_axis=3, concat_axis=0, tiled=True)  14.8 us
    all_to_all x1, starting transfers between devices, local(): lax.all_to_all(block_spec, 'aa', split_axis=3, concat_axis=0, tiled=True)  10.1 us
  transfers between devices with their start and end apart: 3, of which 3 were waited for; matrix products, arithmetic and copies ran while one was open for 0% of the time, Pallas kernels for 0%

commit v1 on v0

--- a/solution.py
+++ b/solution.py
@@ -41,7 +41,7 @@
         FREQS, columns, pts_dev
     )
     product = jnp.einsum("fip,fjp->fij", cols, cols, precision=lax.Precision.HIGHEST)
-    gram_sum = lax.psum(product, ("aa", "ba"))
+    gram_sum = lax.psum(lax.psum(product, "aa"), "ba")
     lower_factor = jnp.linalg.cholesky(gram_sum)
     identity = jnp.broadcast_to(jnp.eye(columns, dtype=gram_sum.dtype), lower_factor.shape)
     inverse = lax.linalg.triangular_solve(lower_factor, identity, left_side=True, lower=True)

time: 479 us -> 436 us (0.910)
  waiting for transfers between devices: 342 us -> 285 us
  blocking collectives: 0 us -> 25 us
  starting transfers between devices: 10.4 us -> 0.3 us
    psum x1 -> x2, waiting for transfers between devices: 247 us -> 205 us  [local(): gram_sum = lax.psum(lax.psum(product, 'aa'), 'ba')]
    all_to_all x0 -> x1, blocking collectives: none -> 25 us  [local(): lax.all_to_all(block_spec, 'aa', split_axis=3, concat_axis=0, tiled=True)]
    all_to_all x1 -> x0, waiting for transfers between devices: 14.8 us -> none  [local(): lax.all_to_all(block_spec, 'aa', split_axis=3, concat_axis=0, tiled=True)]
    all_to_all x1 -> x0, starting transfers between devices: 10.1 us -> none  [local(): lax.all_to_all(block_spec, 'aa', split_axis=3, concat_axis=0, tiled=True)]
    unnamed x3 -> x4, waiting for transfers between devices: 80.2 us -> 80.1 us
where the time goes in v1:
time: 436 us
  waiting for transfers between devices  285 us (65%)
  other arithmetic  88.3 us (20%)
  blocking collectives  25 us (6%)
  between operations  14.5 us (3%)
  matrix products  12.9 us (3%)
  local copies, waits for them, and re-layouts  10.2 us (2%)
    psum x2, waiting for transfers between devices, local(): gram_sum = lax.psum(lax.psum(product, 'aa'), 'ba')  205 us
    unnamed x4, waiting for transfers between devices  80.1 us
    another operation x4, other arithmetic, local(): lower_factor = jnp.linalg.cholesky(gram_sum)  47.1 us
    another operation x2, other arithmetic, local(): lax.linalg.triangular_solve(lower_factor, identity, left_side=True, lower...  39.4 us
    all_to_all x1, blocking collectives, local(): lax.all_to_all(block_spec, 'aa', split_axis=3, concat_axis=0, tiled=True)  25 us
    dot_general x1, matrix products, local(): jnp.einsum('savq,sgf->vgfaq', arranged, table, precision=lax.Precision.HI...  9.16 us
    unnamed x6, local copies, waits for them, and re-layouts  9.1 us
  transfers between devices with their start and end apart: 3, of which 3 were waited for; matrix products, arithmetic and copies ran while one was open for 0% of the time, Pallas kernels for 0%

profile of v1, /device:TPU:2, one launch (start us, length us, event | category | flops | bytes accessed | tf_op | source)
XLA Modules:
  0.0 435.9 jit_solution(16151034163997829041)
XLA Ops:
  7.2 0.0 all-reduce.9.cloned.1.call-start
  7.3 0.6 multiply_reduce_fusion
  8.6 5.9 %copy.38 = f32[4,8,256,256]{3,2,1,0:T(8,128)S(1)} copy(f32[4,8,256,256]{3,1,2,0:T(8,128)} %bitcast.42) | data formatting | bytes 16777216
  14.6 0.1 multiply_multiply_fusion.1
  14.7 9.2 %fusion.3 = f32[8,2,8,32,256]{4,2,0,3,1:T(8,128)} fusion(f32[32,32,8,256]{3,2,1,0:T(8,128)S(1)} %bitcast.41, f32[32,1,8]{0,2,1:T(8,128)S(1)} %get-tuple-element.13, f32[32,1,8]{0,2,1:T(8,128)S(1)} %get-tuple-element.12), kind=kOutput, calls=%fused_computation.3 | convolution fusion | flops 402653696 | bytes 12584960 | tf_op jit(solution)/shard_map/savq,sgf->vgfaq/dot_general | solution.py:35
  23.9 0.0 all-reduce.5.cloned.1.call-start
  24.0 0.6 dynamic-slice
  24.5 80.1 %all-reduce.9.cloned.1.call-done = f32[8,2,8,32,256]{4,2,0,3,1:T(8,128)} async-done(((f32[8,2,8,32,256]{4,2,0,3,1:T(8,128)}), f32[8,2,8,32,256]{4,2,0,3,1:T(8,128)}) %all-reduce.9.cloned.1.call-update) | async-done | bytes 4194320
  104.6 1.7 constant_dynamic-slice_fusion
  106.3 0.1 copy.25
  106.4 25.0 %all_to_all.15 = f32[1,2,8,32,256]{4,2,0,1,3:T(8,128)S(1)} all-to-all(f32[1,2,8,32,256]{4,2,0,1,3:T(8,128)S(1)} %copy.25), channel_id=1, replica_groups=mesh['aa'=32,'ba'=8] {'aa'}, dimensions={3} | all-to-all | bytes 1048576 | tf_op jit(solution)/shard_map/all_to_all | solution.py:37
  131.4 1.6 fusion.7
  133.0 0.2 all-reduce.7.cloned.1.call-start
  133.3 139.1 %all-reduce.5.cloned.1.call-done = f32[8,64,64]{1,2,0:T(8,128)} async-done(((f32[8,64,64]{1,2,0:T(8,128)}), f32[8,64,64]{1,2,0:T(8,128)}) %all-reduce.5.cloned.1.call-update) | async-done | bytes 131088 | tf_op jit(solution)/shard_map/psum | solution.py:44
  272.4 65.4 %all-reduce.7.cloned.1.call-done = f32[8,64,64]{1,2,0:T(8,128)} async-done(((f32[8,64,64]{1,2,0:T(8,128)}), f32[8,64,64]{1,2,0:T(8,128)}) %all-reduce.7.cloned.1.call-update) | async-done | bytes 131088 | tf_op jit(solution)/shard_map/psum | solution.py:44
  337.8 1.1 copy.29
  338.9 1.0 fusion.11
  339.9 46.9 %custom-call.7 = f32[8,64,64]{2,1,0:T(8,128)S(1)} custom-call(f32[8,64,64]{2,1,0:T(8,128)S(1)} %fusion.11), custom_call_target="Cholesky" | custom-call | tf_op jit(solution)/shard_map/jit(cholesky)/cholesky | solution.py:45
  386.9 0.1 compare_reduce_fusion
  387.0 0.1 select_bitcast_fusion
  387.1 39.3 %custom-call.8 = f32[8,1,64,64]{2,3,1,0:T(8,128)S(1)} custom-call(f32[8,1,64,64]{3,2,1,0:T(8,128)S(1)} %get-tuple-element.10), custom_call_target="InvertDiagBlocksLowerTriangular" | custom-call | tf_op jit(solution)/shard_map/triangular_solve | solution.py:47
  426.4 0.6 fusion.9
  427.0 1.5 convolution_multiply_fusion
  428.6 0.8 copy.32
  (12 shorter events, 0.2 us)
Async XLA Ops:
  7.2 97.5 %all-reduce.9.cloned.1.call-start = ((), (), s32[]{:S(2)}) async-start(), calls=%async_computation.3 | async-start | bytes 8388608
  14.7 9.3 %copy-start = (u32[256]{0:T(256)S(1)}, u32[256]{0:T(256)}, u32[]{:S(2)}) copy-start(u32[256]{0:T(256)} %constant.81) | copy-start | bytes 3076
  23.9 248.5 %all-reduce.5.cloned.1.call-start = ((), (), s32[]{:S(2)}) async-start(), calls=%async_computation.1 | async-start | bytes 524288 | tf_op jit(solution)/shard_map/psum | solution.py:44
  133.0 204.8 %all-reduce.7.cloned.1.call-start = ((), (), s32[]{:S(2)}) async-start(), calls=%async_computation.2 | async-start | bytes 524288 | tf_op jit(solution)/shard_map/psum | solution.py:44
Sparse Core Ops, SparseCore 0:
  24.0 80.5 all-reduce.8
  133.1 139.1 all-reduce.4
  274.7 63.1 all-reduce.6
